TPU v7x, 256 devices: a whole 4x4x8 slice. The times are simulated.
256 devices in a mesh: row: 32 (over x, y, core), col: 8 (over z).
Axes of the slice: x: 4, y: 4, z: 8, core: 2. Of those that a mesh axis runs over, the one named last changes fastest.
Arguments:
- matrix: float32 [16384, 16384], P('row', 'col'), may hold values from -9 to 9
- vectors: float32 [16384, 128], P('row'), may hold values from -0.125 to 0.125
- tfactor: float32 [128, 128], replicated, may hold values from -1 to 2, as said below
Outputs:
- updated: float32 [16384, 16384], P('row', 'col')
Inputs may be any that keep to these rules, and one draw needn't show every extreme that they name: tfactor is upper triangular with its diagonal between 0.7 and 1.4.
All inputs are finite; a program needn't handle non-finite values.
Results may differ from a plain program's by a relative error of at most 0.000094.
Values sent between devices are 32-bit elements; how exact they have to be, the bound alone decides.
No kernel may reach another device: no remote copies, remote signals or barrier semaphores. Data moves between devices by JAX's collectives and lax.ppermute only.
A program may use at most 128 MiB of HBM per device.

v0:
```python
import jax
import jax.numpy as jnp
from jax import lax
from jax.sharding import PartitionSpec as P


def product(left, right):
    return jnp.dot(left, right, precision=lax.Precision.HIGHEST, preferred_element_type=jnp.float32)


def inner_product(left, right):
    return lax.dot_general(
        left,
        right,
        (((0,), (0,)), ((), ())),
        precision=lax.Precision.HIGHEST,
        preferred_element_type=jnp.float32,
    )


def outer_product(left, right):
    return lax.dot_general(
        left,
        right,
        (((1,), (1,)), ((), ())),
        precision=lax.Precision.HIGHEST,
        preferred_element_type=jnp.float32,
    )


def to_columns(panel_rows):
    rows_here = panel_rows.shape[0]
    row_count = lax.axis_size("row")
    blocks_per = row_count // lax.axis_size("col")
    col_index = lax.axis_index("col")
    gathered = lax.all_gather(panel_rows, "row", axis=0, tiled=True)
    return lax.dynamic_slice_in_dim(
        gathered, col_index * (blocks_per * rows_here), blocks_per * rows_here, 0
    )


def shards(matrix, vectors, tfactor):
    vec_cols = to_columns(vectors)
    x_rows = lax.psum(product(matrix, vec_cols), "col")
    y_rows = product(x_rows, tfactor)
    cross_terms = lax.psum(inner_product(vectors, y_rows), "row")
    coupling = inner_product(tfactor, cross_terms)
    w_rows = y_rows - 0.5 * product(vectors, coupling)
    w_cols = to_columns(w_rows)
    return matrix - outer_product(vectors, w_cols) - outer_product(w_rows, vec_cols)


def solution(mesh):
    in_specs = (P("row", "col"), P("row", None), P())
    out_specs = P("row", "col")
    return jax.shard_map(shards, mesh=mesh, in_specs=in_specs, out_specs=out_specs, check_vma=False)
```

profile of v0, /device:TPU:1, one launch (start us, length us, event | category | flops | bytes accessed | tf_op | source)
XLA Modules:
  0.0 338.5 jit_solution(5405151360092062463)
XLA Ops:
  6.5 0.0 copy-start
  6.5 0.0 all-gather.3.cloned.1.call-start
  6.5 0.7 all-gather.3.cloned.1.call-update
  7.3 0.0 all-reduce.3.cloned.1.call-start
  7.3 64.8 %all-gather.3.cloned.1.call-done = f32[16384,128]{1,0:T(8,128)} async-done(((f32[512,128]{1,0:T(8,128)}), f32[16384,128]{1,0:T(8,128)}) %all-gather.3.cloned.1.call-update) | async-done | bytes 8388624 | tf_op jit(solution)/shard_map/all_gather | solution.py:36
  72.1 7.7 %convolution_bitcast_fusion = f32[512,128]{0,1:T(8,128)} fusion(f32[512,2048]{1,0:T(8,128)} %param.3, f32[16384,128]{1,0:T(8,128)} %all-gather.3.cloned.1.call-done, s32[]{:T(128)S(6)} %select_n.4), kind=kOutput, calls=%fused_computation.5 | convolution fusion | flops 1610612736 | bytes 5505028 | tf_op jit(solution)/shard_map/dot_general | solution.py:8
  79.7 0.0 all-reduce.3.cloned.1.call-update
  79.8 0.0 all-reduce.5.cloned.1.call-start
  79.8 67.3 %all-reduce.3.cloned.1.call-done = f32[512,128]{0,1:T(8,128)} async-done(((f32[512,128]{0,1:T(8,128)}), f32[512,128]{0,1:T(8,128)}) %all-reduce.3.cloned.1.call-update) | async-done | bytes 262160 | tf_op jit(solution)/shard_map/psum | solution.py:44
  147.1 0.0 copy-done
  147.1 1.5 fusion.10
  148.6 0.0 copy-done.1
  148.7 1.2 convolution_bitcast_fusion.1
  149.9 0.0 all-reduce.5.cloned.1.call-update
  149.9 0.0 all-gather.5.cloned.1.call-start
  150.0 109.7 %all-reduce.5.cloned.1.call-done = f32[128,128]{0,1:T(8,128)} async-done(((f32[128,128]{0,1:T(8,128)}), f32[128,128]{0,1:T(8,128)}) %all-reduce.5.cloned.1.call-update) | async-done | bytes 65552 | tf_op jit(solution)/shard_map/psum | solution.py:46
  259.7 1.0 fusion.11
  260.7 1.1 fusion.2
  261.8 0.0 all-gather.5.cloned.1.call-update
  261.8 5.4 %copy.5 = f32[512,2048]{0,1:T(8,128)} copy(f32[512,2048]{1,0:T(8,128)} %param.3) | data formatting | bytes 8388608 | tf_op args[0]
  267.2 6.2 %fusion.4 = f32[512,2048]{0,1:T(8,128)} fusion(f32[512,128]{1,0:T(8,128)S(1)} %copy-done.2, f32[16384,128]{1,0:T(8,128)} %all-gather.3.cloned.1.call-done, s32[]{:T(128)S(6)} %select_n.4), kind=kOutput, calls=%fused_computation.8 | convolution fusion | flops 1610612736 | bytes 5505028 | tf_op jit(solution)/shard_map/dot_general | solution.py:22
  273.4 45.7 %all-gather.5.cloned.1.call-done = f32[16384,128]{1,0:T(8,128)} async-done(((f32[512,128]{1,0:T(8,128)}), f32[16384,128]{1,0:T(8,128)}) %all-gather.5.cloned.1.call-update) | async-done | bytes 8388624 | tf_op jit(solution)/shard_map/all_gather | solution.py:36
  319.1 7.5 %fusion = f32[512,2048]{0,1:T(8,128)} fusion(f32[512,2048]{0,1:T(8,128)} %fusion.4, f32[512,2048]{0,1:T(8,128)} %copy.5, f32[512,128]{1,0:T(8,128)S(1)} %copy-done.1, f32[16384,128]{1,0:T(8,128)} %all-gather.5.cloned.1.call-done, s32[]{:T(128)S(6)} %select_n.4), kind=kOutput, calls=%fused_computation.1 | convolution fusion | flops 1612709888 | bytes 13893636 | tf_op jit(solution)/shard_map/dot_general | solution.py:22
  326.6 5.3 %copy.7 = f32[512,2048]{1,0:T(8,128)} copy(f32[512,2048]{0,1:T(8,128)} %fusion) | data formatting | bytes 8388608 | tf_op jit(solution)/shard_map/sub | solution.py:50
  (3 shorter events, 0.0 us)
Async XLA Ops:
  6.5 140.6 %copy-start = (f32[128,128]{1,0:T(8,128)S(1)}, f32[128,128]{1,0:T(8,128)}, u32[]{:S(2)}) copy-start(f32[128,128]{1,0:T(8,128)} %param.5) | copy-start | bytes 196612
  6.5 142.1 %copy-start.1 = (f32[512,128]{1,0:T(8,128)S(1)}, f32[512,128]{1,0:T(8,128)}, u32[]{:S(2)}) copy-start(f32[512,128]{1,0:T(8,128)} %param.4) | copy-start | bytes 786436
  6.5 65.5 %all-gather.3.cloned.1.call-start = ((), (), s32[]{:S(2)}) async-start(), calls=%async_computation | async-start | bytes 8650752 | tf_op jit(solution)/shard_map/all_gather | solution.py:36
  7.3 139.8 %all-reduce.3.cloned.1.call-start = ((), (), s32[]{:S(2)}) async-start(), calls=%async_computation.1 | async-start | bytes 524288 | tf_op jit(solution)/shard_map/psum | solution.py:44
  79.8 179.9 %all-reduce.5.cloned.1.call-start = ((), (), s32[]{:S(2)}) async-start(), calls=%async_computation.2 | async-start | bytes 131072 | tf_op jit(solution)/shard_map/psum | solution.py:46
  149.9 169.2 %all-gather.5.cloned.1.call-start = ((), (), s32[]{:S(2)}) async-start(), calls=%async_computation.3 | async-start | bytes 8650752 | tf_op jit(solution)/shard_map/all_gather | solution.py:36
  261.8 5.4 %copy-start.2 = (f32[512,128]{1,0:T(8,128)S(1)}, f32[512,128]{1,0:T(8,128)}, u32[]{:S(2)}) copy-start(f32[512,128]{1,0:T(8,128)} %fusion.2) | copy-start | bytes 786436
Sparse Core Ops, SparseCore 0:
  9.9 62.1 all-gather.2
  79.9 67.1 all-reduce.2
  150.7 108.9 all-reduce.4
  262.1 56.9 all-gather.4
where the time goes:
time: 339 us
  waiting for transfers between devices  288 us (85%)
  matrix products  26.2 us (8%)
  between operations  13.2 us (4%)
  local copies, waits for them, and re-layouts  10.8 us (3%)
    all_gather x2, waiting for transfers between devices, to_columns(): gathered = lax.all_gather(panel_rows, 'row', axis=0, tiled=True)  110 us
    psum x1, waiting for transfers between devices, shards(): cross_terms = lax.psum(inner_product(vectors, y_rows), 'row')  110 us
    psum x1, waiting for transfers between devices, shards(): x_rows = lax.psum(product(matrix, vec_cols), 'col')  67.3 us
    dot_general x2, matrix products, outer_product(): lax.dot_general(left, right, (((1,), (1,)), ((), ())), precision=lax.Prec...  13.7 us
    dot_general x3, matrix products, product(): jnp.dot(left, right, precision=lax.Precision.HIGHEST, preferred_element_t...  10.3 us
  transfers between devices with their start and end apart: 4, of which 4 were waited for; matrix products, arithmetic and copies ran while one was open for 3% of the time, Pallas kernels for 0%

commit v1 on v0

--- a/solution.py
+++ b/solution.py
@@ -33,7 +33,9 @@
     row_count = lax.axis_size("row")
     blocks_per = row_count // lax.axis_size("col")
     col_index = lax.axis_index("col")
-    gathered = lax.all_gather(panel_rows, "row", axis=0, tiled=True)
+    gathered = jnp.concatenate(
+        lax.all_to_all(jnp.stack([panel_rows] * lax.axis_size("row")), "row", 0, 0), axis=0
+    )
     return lax.dynamic_slice_in_dim(
         gathered, col_index * (blocks_per * rows_here), blocks_per * rows_here, 0
     )

time: 339 us -> 489 us (1.44)
  the two profiles are of different devices: /device:TPU:1 before, /device:TPU:44 now
where the time goes in v1:
time: 489 us
  waiting for transfers between devices  416 us (85%)
  matrix products  25.5 us (5%)
  local copies, waits for them, and re-layouts  20.1 us (4%)
  starting transfers between devices  13.8 us (3%)
  between operations  13.5 us (3%)
    all_to_all x2, waiting for transfers between devices, to_columns(): lax.all_to_all(jnp.stack([panel_rows] * lax.axis_size('row')), 'row', 0, 0)  239 us
    psum x1, waiting for transfers between devices, shards(): cross_terms = lax.psum(inner_product(vectors, y_rows), 'row')  104 us
    psum x1, waiting for transfers between devices, shards(): x_rows = lax.psum(product(matrix, vec_cols), 'col')  73.3 us
    all_to_all x2, starting transfers between devices, to_columns(): lax.all_to_all(jnp.stack([panel_rows] * lax.axis_size('row')), 'row', 0, 0)  13.7 us
    dot_general x2, matrix products, outer_product(): lax.dot_general(left, right, (((1,), (1,)), ((), ())), precision=lax.Prec...  13.6 us
  transfers between devices with their start and end apart: 4, of which 4 were waited for; matrix products, arithmetic and copies ran while one was open for 2% of the time, Pallas kernels for 0%

profile of v1, /device:TPU:44, one launch (start us, length us, event | category | flops | bytes accessed | tf_op | source)
XLA Modules:
  0.0 488.9 jit_solution(15407347782724344737)
XLA Ops:
  6.5 0.0 copy-start
  6.5 5.2 %stack.4 = f32[32,512,128]{2,1,0:T(8,128)} broadcast(f32[512,128]{1,0:T(8,128)} %param.4), dimensions={1,2} | broadcast | bytes 8650752 | tf_op jit(solution)/shard_map/stack | solution.py:37
  11.7 7.5 %all-to-all-start = ((f32[32,512,128]{2,1,0:T(8,128)}), f32[32,512,128]{2,1,0:T(8,128)}, u32[]{:S(2)}, u32[]{:S(2)}) async-start(f32[32,512,128]{2,1,0:T(8,128)} %stack.4), calls=%async_computation | async-start | bytes 16777216 | tf_op jit(solution)/shard_map/all_to_all | solution.py:37
  19.2 0.0 copy-start.1
  19.3 0.0 all-reduce.3.cloned.1.call-start
  19.3 124.0 %all-to-all-done = f32[32,512,128]{2,1,0:T(8,128)} async-done(((f32[32,512,128]{2,1,0:T(8,128)}), f32[32,512,128]{2,1,0:T(8,128)}, u32[]{:S(2)}, u32[]{:S(2)}) %all-to-all-start) | async-done | bytes 8388640 | tf_op jit(solution)/shard_map/all_to_all | solution.py:37
  143.3 7.7 %convolution_bitcast_fusion = f32[512,128]{0,1:T(8,128)} fusion(f32[512,2048]{1,0:T(8,128)} %param.3, f32[16384,128]{1,0:T(8,128)} %bitcast, s32[]{:T(128)S(6)} %select_n.4), kind=kOutput, calls=%fused_computation.5 | convolution fusion | flops 1610612736 | bytes 5505028 | tf_op jit(solution)/shard_map/dot_general | solution.py:8
  151.0 0.0 all-reduce.3.cloned.1.call-update
  151.0 0.0 all-reduce.5.cloned.1.call-start
  151.1 73.3 %all-reduce.3.cloned.1.call-done = f32[512,128]{0,1:T(8,128)} async-done(((f32[512,128]{0,1:T(8,128)}), f32[512,128]{0,1:T(8,128)}) %all-reduce.3.cloned.1.call-update) | async-done | bytes 262160 | tf_op jit(solution)/shard_map/psum | solution.py:46
  224.3 0.0 copy-done
  224.3 1.5 fusion.10
  225.9 1.2 convolution_bitcast_fusion.1
  227.1 0.0 all-reduce.5.cloned.1.call-update
  227.1 104.3 %all-reduce.5.cloned.1.call-done = f32[128,128]{0,1:T(8,128)} async-done(((f32[128,128]{0,1:T(8,128)}), f32[128,128]{0,1:T(8,128)}) %all-reduce.5.cloned.1.call-update) | async-done | bytes 65552 | tf_op jit(solution)/shard_map/psum | solution.py:48
  331.5 1.0 fusion.11
  332.5 0.4 fusion.2
  332.9 4.2 stack.5
  337.1 6.1 %all-to-all-start.1 = ((f32[32,512,128]{2,1,0:T(8,128)}), f32[32,512,128]{2,1,0:T(8,128)}, u32[]{:S(2)}, u32[]{:S(2)}) async-start(f32[32,512,128]{2,1,0:T(8,128)} %stack.5), calls=%async_computation.1 | async-start | bytes 16777216 | tf_op jit(solution)/shard_map/all_to_all | solution.py:37
  343.2 5.4 %copy.5 = f32[512,2048]{0,1:T(8,128)} copy(f32[512,2048]{1,0:T(8,128)} %param.3) | data formatting | bytes 8388608 | tf_op args[0]
  348.6 6.2 %fusion.4 = f32[512,2048]{0,1:T(8,128)} fusion(f32[512,128]{1,0:T(8,128)S(1)} %fusion.2, f32[16384,128]{1,0:T(8,128)} %bitcast, s32[]{:T(128)S(6)} %select_n.4), kind=kOutput, calls=%fused_computation.8 | convolution fusion | flops 1610612736 | bytes 5505028 | tf_op jit(solution)/shard_map/dot_general | solution.py:22
  354.8 114.5 %all-to-all-done.1 = f32[32,512,128]{2,1,0:T(8,128)} async-done(((f32[32,512,128]{2,1,0:T(8,128)}), f32[32,512,128]{2,1,0:T(8,128)}, u32[]{:S(2)}, u32[]{:S(2)}) %all-to-all-start.1) | async-done | bytes 8388640 | tf_op jit(solution)/shard_map/all_to_all | solution.py:37
  469.2 7.5 %fusion = f32[512,2048]{0,1:T(8,128)} fusion(f32[512,2048]{0,1:T(8,128)} %fusion.4, f32[512,2048]{0,1:T(8,128)} %copy.5, f32[512,128]{1,0:T(8,128)S(1)} %copy-done.1, f32[16384,128]{1,0:T(8,128)} %bitcast.4, s32[]{:T(128)S(6)} %select_n.4), kind=kOutput, calls=%fused_computation.1 | convolution fusion | flops 1612709888 | bytes 13893636 | tf_op jit(solution)/shard_map/dot_general | solution.py:22
  476.7 5.3 %copy.7 = f32[512,2048]{1,0:T(8,128)} copy(f32[512,2048]{0,1:T(8,128)} %fusion) | data formatting | bytes 8388608 | tf_op jit(solution)/shard_map/sub | solution.py:52
  (1 shorter events, 0.0 us)
Async XLA Ops:
  6.5 217.8 %copy-start = (f32[128,128]{1,0:T(8,128)S(1)}, f32[128,128]{1,0:T(8,128)}, u32[]{:S(2)}) copy-start(f32[128,128]{1,0:T(8,128)} %param.5) | copy-start | bytes 196612
  11.7 131.6 %all-to-all-start = ((f32[32,512,128]{2,1,0:T(8,128)}), f32[32,512,128]{2,1,0:T(8,128)}, u32[]{:S(2)}, u32[]{:S(2)}) async-start(f32[32,512,128]{2,1,0:T(8,128)} %stack.4), calls=%async_computation | async-start | bytes 16777216 | tf_op jit(solution)/shard_map/all_to_all | solution.py:37
  19.2 206.6 %copy-start.1 = (f32[512,128]{1,0:T(8,128)S(1)}, f32[512,128]{1,0:T(8,128)}, u32[]{:S(2)}) copy-start(f32[512,128]{1,0:T(8,128)} %param.4) | copy-start | bytes 786436
  19.3 205.1 %all-reduce.3.cloned.1.call-start = ((), (), s32[]{:S(2)}) async-start(), calls=%async_computation.2 | async-start | bytes 524288 | tf_op jit(solution)/shard_map/psum | solution.py:46
  151.0 180.4 %all-reduce.5.cloned.1.call-start = ((), (), s32[]{:S(2)}) async-start(), calls=%async_computation.3 | async-start | bytes 131072 | tf_op jit(solution)/shard_map/psum | solution.py:48
  337.1 132.2 %all-to-all-start.1 = ((f32[32,512,128]{2,1,0:T(8,128)}), f32[32,512,128]{2,1,0:T(8,128)}, u32[]{:S(2)}, u32[]{:S(2)}) async-start(f32[32,512,128]{2,1,0:T(8,128)} %stack.5), calls=%async_computation.1 | async-start | bytes 16777216 | tf_op jit(solution)/shard_map/all_to_all | solution.py:37
Sparse Core Ops, SparseCore 0:
  151.1 73.1 all-reduce.2
  227.9 103.4 all-reduce.4

commit v2 on v0

--- a/solution.py
+++ b/solution.py
@@ -43,7 +43,7 @@
     vec_cols = to_columns(vectors)
     x_rows = lax.psum(product(matrix, vec_cols), "col")
     y_rows = product(x_rows, tfactor)
-    cross_terms = lax.psum(inner_product(vectors, y_rows), "row")
+    cross_terms = jnp.sum(lax.all_gather(inner_product(vectors, y_rows), "row"), axis=0)
     coupling = inner_product(tfactor, cross_terms)
     w_rows = y_rows - 0.5 * product(vectors, coupling)
     w_cols = to_columns(w_rows)

time: 339 us -> 284 us (0.84)
  waiting for transfers between devices: 288 us -> 232 us
    psum x1 -> x0, waiting for transfers between devices: 110 us -> none  [shards(): cross_terms = lax.psum(inner_product(vectors, y_rows), 'row')]
    all_gather x0 -> x1, waiting for transfers between devices: none -> 53.2 us  [shards(): lax.all_gather(inner_product(vectors, y_rows), 'row')]
    unnamed x7 -> x8, local copies, waits for them, and re-layouts: 5.43 us -> 7.38 us
  transfers between devices with their start and end apart: 4 -> 4, of which waited for: 4 -> 4; matrix products, arithmetic and copies ran while one was open for 3% -> 4% of each run, Pallas kernels for 0% -> 0%
where the time goes in v2:
time: 284 us
  waiting for transfers between devices  232 us (82%)
  matrix products  25.4 us (9%)
  between operations  13.2 us (5%)
  local copies, waits for them, and re-layouts  12.7 us (4%)
    all_gather x2, waiting for transfers between devices, to_columns(): gathered = lax.all_gather(panel_rows, 'row', axis=0, tiled=True)  111 us
    psum x1, waiting for transfers between devices, shards(): x_rows = lax.psum(product(matrix, vec_cols), 'col')  67.3 us
    all_gather x1, waiting for transfers between devices, shards(): lax.all_gather(inner_product(vectors, y_rows), 'row')  53.2 us
    dot_general x2, matrix products, outer_product(): lax.dot_general(left, right, (((1,), (1,)), ((), ())), precision=lax.Prec...  13.7 us
    dot_general x3, matrix products, product(): jnp.dot(left, right, precision=lax.Precision.HIGHEST, preferred_element_t...  10.3 us
    unnamed x8, local copies, waits for them, and re-layouts  7.38 us
  transfers between devices with their start and end apart: 4, of which 4 were waited for; matrix products, arithmetic and copies ran while one was open for 4% of the time, Pallas kernels for 0%

profile of v2, /device:TPU:1, one launch (start us, length us, event | category | flops | bytes accessed | tf_op | source)
XLA Modules:
  0.0 283.6 jit_solution(14636713255522737675)
XLA Ops:
  6.5 0.7 all-gather.5.cloned.1.call-update
  7.3 0.0 all-reduce.2.cloned.1.call-start
  7.3 64.8 %all-gather.5.cloned.1.call-done = f32[16384,128]{1,0:T(8,128)} async-done(((f32[512,128]{1,0:T(8,128)}), f32[16384,128]{1,0:T(8,128)}) %all-gather.5.cloned.1.call-update) | async-done | bytes 8388624 | tf_op jit(solution)/shard_map/all_gather | solution.py:36
  72.1 7.7 %convolution_bitcast_fusion = f32[512,128]{0,1:T(8,128)} fusion(f32[512,2048]{1,0:T(8,128)} %param.3, f32[16384,128]{1,0:T(8,128)} %all-gather.5.cloned.1.call-done, s32[]{:T(128)S(6)} %select_n.4), kind=kOutput, calls=%fused_computation.6 | convolution fusion | flops 1610612736 | bytes 5505028 | tf_op jit(solution)/shard_map/dot_general | solution.py:8
  79.7 0.0 all-reduce.2.cloned.1.call-update
  79.8 0.0 all-gather.9.cloned.1.call-start
  79.8 67.3 %all-reduce.2.cloned.1.call-done = f32[512,128]{0,1:T(8,128)} async-done(((f32[512,128]{0,1:T(8,128)}), f32[512,128]{0,1:T(8,128)}) %all-reduce.2.cloned.1.call-update) | async-done | bytes 262160 | tf_op jit(solution)/shard_map/psum | solution.py:44
  147.1 0.0 copy-done
  147.1 1.5 fusion.10
  148.7 1.2 convolution_bitcast_fusion.1
  149.9 0.0 all-gather.9.cloned.1.call-update
  149.9 0.0 all-gather.7.cloned.1.call-start
  150.0 53.2 %all-gather.9.cloned.1.call-done = f32[4096,128]{0,1:T(8,128)} async-done(((f32[128,128]{0,1:T(8,128)}), f32[4096,128]{0,1:T(8,128)}) %all-gather.9.cloned.1.call-update) | async-done | bytes 2097168 | tf_op jit(solution)/shard_map/all_gather | solution.py:46
  203.2 2.0 copy.14
  205.1 0.2 bitcast_reduce_fusion
  205.4 0.2 fusion.11
  205.6 1.1 fusion.2
  206.7 0.0 all-gather.7.cloned.1.call-update
  206.7 5.4 %copy.9 = f32[512,2048]{0,1:T(8,128)} copy(f32[512,2048]{1,0:T(8,128)} %param.3) | data formatting | bytes 8388608 | tf_op args[0]
  212.1 0.0 copy-done.2
  212.1 6.2 %fusion.4 = f32[512,2048]{0,1:T(8,128)} fusion(f32[512,128]{1,0:T(8,128)S(1)} %copy-done.2, f32[16384,128]{1,0:T(8,128)} %all-gather.5.cloned.1.call-done, s32[]{:T(128)S(6)} %select_n.4), kind=kOutput, calls=%fused_computation.9 | convolution fusion | flops 1610612736 | bytes 5505028 | tf_op jit(solution)/shard_map/dot_general | solution.py:22
  218.3 46.0 %all-gather.7.cloned.1.call-done = f32[16384,128]{1,0:T(8,128)} async-done(((f32[512,128]{1,0:T(8,128)}), f32[16384,128]{1,0:T(8,128)}) %all-gather.7.cloned.1.call-update) | async-done | bytes 8388624 | tf_op jit(solution)/shard_map/all_gather | solution.py:36
  264.2 7.5 %fusion = f32[512,2048]{0,1:T(8,128)} fusion(f32[512,2048]{0,1:T(8,128)} %fusion.4, f32[512,2048]{0,1:T(8,128)} %copy.9, f32[512,128]{1,0:T(8,128)S(1)} %copy-done.1, f32[16384,128]{1,0:T(8,128)} %all-gather.7.cloned.1.call-done, s32[]{:T(128)S(6)} %select_n.4), kind=kOutput, calls=%fused_computation.1 | convolution fusion | flops 1612709888 | bytes 13893636 | tf_op jit(solution)/shard_map/dot_general | solution.py:22
  271.8 5.3 %copy.11 = f32[512,2048]{1,0:T(8,128)} copy(f32[512,2048]{0,1:T(8,128)} %fusion) | data formatting | bytes 8388608 | tf_op jit(solution)/shard_map/sub | solution.py:50
  (5 shorter events, 0.0 us)
Async XLA Ops:
  6.5 140.6 %copy-start = (f32[128,128]{1,0:T(8,128)S(1)}, f32[128,128]{1,0:T(8,128)}, u32[]{:S(2)}) copy-start(f32[128,128]{1,0:T(8,128)} %param.5) | copy-start | bytes 196612
  6.5 142.1 %copy-start.1 = (f32[512,128]{1,0:T(8,128)S(1)}, f32[512,128]{1,0:T(8,128)}, u32[]{:S(2)}) copy-start(f32[512,128]{1,0:T(8,128)} %param.4) | copy-start | bytes 786436
  6.5 65.5 %all-gather.5.cloned.1.call-start = ((), (), s32[]{:S(2)}) async-start(), calls=%async_computation | async-start | bytes 8650752 | tf_op jit(solution)/shard_map/all_gather | solution.py:36
  7.3 139.8 %all-reduce.2.cloned.1.call-start = ((), (), s32[]{:S(2)}) async-start(), calls=%async_computation.1 | async-start | bytes 524288 | tf_op jit(solution)/shard_map/psum | solution.py:44
  79.8 123.4 %all-gather.9.cloned.1.call-start = ((), (), s32[]{:S(2)}) async-start(), calls=%async_computation.3 | async-start | bytes 2162688 | tf_op jit(solution)/shard_map/all_gather | solution.py:46
  149.9 114.3 %all-gather.7.cloned.1.call-start = ((), (), s32[]{:S(2)}) async-start(), calls=%async_computation.2 | async-start | bytes 8650752 | tf_op jit(solution)/shard_map/all_gather | solution.py:36
  206.7 5.4 %copy-start.2 = (f32[512,128]{1,0:T(8,128)S(1)}, f32[512,128]{1,0:T(8,128)}, u32[]{:S(2)}) copy-start(f32[512,128]{1,0:T(8,128)} %fusion.2) | copy-start | bytes 786436
Sparse Core Ops, SparseCore 0:
  9.9 62.1 all-gather.4
  79.9 67.1 all-reduce.1
  150.0 53.1 all-gather.8
  206.8 57.3 all-gather.6
